TPU v7x, 128 devices: a whole 4x4x4 slice. The times are simulated.
128 devices in a mesh: ctx: 16 (over y_lo, z, core), head: 8 (over x, y_hi).
Axes of the slice: x: 4, y: 4 (y_hi: 2, y_lo: 2; y = y_hi * 2 + y_lo), z: 4, core: 2. Of those that a mesh axis runs over, the one named last changes fastest.
Arguments:
- hidden_in: bfloat16 [4096, 8192], P('ctx', 'head'), may hold values from -90 to 90
- query_rows: bfloat16 [4096, 8192], P('ctx', 'head'), may hold values from -5 to 5
- key_rows: bfloat16 [4096, 1024], P('ctx', 'head'), may hold values from -5 to 5
- value_rows: bfloat16 [4096, 1024], P('ctx', 'head'), may hold values from -6 to 6
- out_weight: bfloat16 [8192, 8192], P('head'), may hold values from -0.0625 to 0.0625
- grad_out: bfloat16 [4096, 8192], P('ctx', 'head'), may hold values from -6 to 6
- answer_mask: int32 [4096], P('ctx'), may hold values 0 or 1
Outputs:
- grad_query: bfloat16 [4096, 8192], P('ctx', 'head')
- grad_key: bfloat16 [4096, 1024], P('ctx', 'head')
- grad_value: bfloat16 [4096, 1024], P('ctx', 'head')
- fisher_q: float32 [16, 64], P('ctx', 'head')
- fisher_o: float32 [16, 64], P('ctx', 'head')
All inputs are finite; a program needn't handle non-finite values. No bound on the sum of `answer_mask` on one device may be relied on, other than what follows from the above.
Results may differ from a plain program's by a relative error of at most 0.019.
Values may be sent and summed in bfloat16 or wider, within the bound.
No kernel may reach another device: no remote copies, remote signals or barrier semaphores. Data moves between devices by JAX's collectives and lax.ppermute only.
A program may use at most 128 MiB of HBM per device.

v0:
```python
import math
import jax
import jax.numpy as jnp
from jax import lax
from jax.sharding import PartitionSpec as P

D = 8192
HEADS = 64
KVH = 8
HD = 128
NEGATIVE = -1e30
EPSILON = 1e-06


def block_scores(query_group, key_block, scaling, row_pos, col_pos):
    scores = (
        jnp.einsum("tgd,kd->tgk", query_group, key_block, preferred_element_type=jnp.float32)
        * scaling
    )
    return jnp.where(row_pos[:, None, None] >= col_pos[None, None, :], scores, NEGATIVE)


def head_squares(left_side, right_side, head_dim):
    product = lax.dot_general(
        left_side, right_side, (((0,), (0,)), ((), ())), preferred_element_type=jnp.float32
    )
    shaped = (product * product).reshape(
        product.shape[0], right_side.shape[1] // head_dim, head_dim
    )
    return jnp.sum(shaped, axis=(0, 2))


def gram_pair_squares(left_gram, right_side, head_dim):
    rows = right_side.shape[0]
    right_heads = right_side.reshape(rows, right_side.shape[1] // head_dim, head_dim)
    right_gram = jnp.einsum(
        "ihd,jhd->hij", right_heads, right_heads, preferred_element_type=jnp.float32
    )
    return jnp.sum(right_gram * left_gram[None], axis=(1, 2))


def gram_squares(left_side, right_side, head_dim):
    left_gram = lax.dot_general(
        left_side, left_side, (((1,), (1,)), ((), ())), preferred_element_type=jnp.float32
    )
    return gram_pair_squares(left_gram, right_side, head_dim)


def body(hidden_in, query_rows, key_rows, value_rows, out_weight, grad_out, answer_mask):
    tok_dev = query_rows.shape[0]
    head_dim = HD
    group_size = HEADS // KVH
    local_groups = key_rows.shape[1] // head_dim
    scaling = head_dim ** (-0.5)
    own_index = lax.axis_index("ctx")
    first_row = own_index * tok_dev
    loss_weight = 0.25 + answer_mask.astype(jnp.float32)
    weighted = (grad_out.astype(jnp.float32) * loss_weight[:, None]).astype(jnp.bfloat16)
    hidden_gram = lax.psum(
        lax.dot_general(
            hidden_in, hidden_in, (((1,), (1,)), ((), ())), preferred_element_type=jnp.float32
        ),
        "head",
    )
    pair_all = lax.all_gather(
        jnp.concatenate([key_rows, value_rows], axis=1), "ctx", axis=0, tiled=True
    )
    kv_width = key_rows.shape[1]
    keys_all, values_all = (pair_all[:, :kv_width], pair_all[:, kv_width:])
    tokens = keys_all.shape[0]
    block_rows = math.gcd(512, tokens)

    def fetch(table, block_number):
        return lax.dynamic_slice_in_dim(table, block_number * block_rows, block_rows, 0)

    def column_pos(block_number):
        return block_number * block_rows + jnp.arange(block_rows, dtype=jnp.int32)

    buffer = jnp.zeros((tokens, 2 * local_groups * head_dim), jnp.float32)
    rows = query_rows.shape[0]
    row_pos = first_row + jnp.arange(rows, dtype=jnp.int32)
    needed = (first_row + rows - 1) // block_rows + 1
    query_heads = query_rows.reshape(rows, local_groups, group_size, head_dim)
    log_totals = []
    shared_head = 0
    query_group = query_heads[:, shared_head]

    def stats_step(block_number, carried):
        running_max, running_sum = carried
        key_block = fetch(keys_all, block_number)
        scores = block_scores(query_group, key_block, scaling, row_pos, column_pos(block_number))
        new_max = jnp.maximum(running_max, jnp.max(scores, axis=-1))
        running_sum = running_sum * jnp.exp(running_max - new_max) + jnp.sum(
            jnp.exp(scores - new_max[..., None]), axis=-1
        )
        return (new_max, running_sum)

    start_max = jnp.full((rows, group_size), NEGATIVE, jnp.float32)
    start_sum = jnp.zeros((rows, group_size), jnp.float32)
    running_max, running_sum = lax.fori_loop(0, needed, stats_step, (start_max, start_sum))
    log_total = running_max + jnp.log(running_sum)

    def value_step(block_number, accumulated):
        key_block = fetch(keys_all, block_number)
        value_block = fetch(values_all, block_number)
        scores = block_scores(query_group, key_block, scaling, row_pos, column_pos(block_number))
        rounded = jnp.exp(scores - log_total[..., None]).astype(jnp.bfloat16)
        return accumulated + jnp.einsum(
            "tgk,kd->tgd", rounded, value_block, preferred_element_type=jnp.float32
        )

    accumulated = lax.fori_loop(
        0, needed, value_step, jnp.zeros((rows, group_size, head_dim), jnp.float32)
    )
    log_totals.append(log_total)
    attended_list = [accumulated.astype(jnp.bfloat16)]
    attended_part = jnp.stack(attended_list, axis=1).reshape(
        rows, local_groups * group_size * head_dim
    )
    log_totals, attended = (log_totals, attended_part)
    piece_part = lax.all_gather(weighted, "head", axis=1, tiled=True)
    grad_sum = lax.dot_general(
        piece_part, out_weight, (((1,), (1,)), ((), ())), preferred_element_type=jnp.float32
    )
    grad_sum, squares_out = (grad_sum, gram_squares(piece_part, attended, head_dim))
    grad_attended, squares_out = (grad_sum.astype(jnp.bfloat16), squares_out)
    backward_buffer = buffer
    rows = query_rows.shape[0]
    backward_row_pos = first_row + jnp.arange(rows, dtype=jnp.int32)
    needed = (first_row + rows - 1) // block_rows + 1
    query_heads = query_rows.reshape(rows, local_groups, group_size, head_dim)
    grad_heads = grad_attended.reshape(rows, local_groups, group_size, head_dim)
    attended_heads = attended.reshape(rows, local_groups, group_size, head_dim)
    shared_head = 0
    backward_query_group = query_heads[:, shared_head]
    grad_group = grad_heads[:, shared_head]
    backward_log_total = log_totals[shared_head]
    row_dot = jnp.sum(
        grad_group.astype(jnp.float32) * attended_heads[:, shared_head].astype(jnp.float32), axis=-1
    )
    key_column = jnp.int32(shared_head * head_dim)
    value_column = jnp.int32((local_groups + shared_head) * head_dim)

    def back_step(block_number, carried):
        query_sum, buffer_now = carried
        key_block = fetch(keys_all, block_number)
        value_block = fetch(values_all, block_number)
        scores = block_scores(
            backward_query_group, key_block, scaling, backward_row_pos, column_pos(block_number)
        )
        softmax = jnp.exp(scores - backward_log_total[..., None])
        rounded = softmax.astype(jnp.bfloat16)
        grad_prob = jnp.einsum(
            "tgd,kd->tgk", grad_group, value_block, preferred_element_type=jnp.float32
        )
        grad_score = (softmax * (grad_prob - row_dot[..., None]) * scaling).astype(jnp.bfloat16)
        query_sum = query_sum + jnp.einsum(
            "tgk,kd->tgd", grad_score, key_block, preferred_element_type=jnp.float32
        )
        key_part = jnp.einsum(
            "tgk,tgd->kd", grad_score, backward_query_group, preferred_element_type=jnp.float32
        )
        value_part = jnp.einsum(
            "tgk,tgd->kd", rounded, grad_group, preferred_element_type=jnp.float32
        )
        row_start = (block_number * block_rows).astype(jnp.int32)
        old_key = lax.dynamic_slice(buffer_now, (row_start, key_column), (block_rows, head_dim))
        buffer_now = lax.dynamic_update_slice(
            buffer_now, old_key + key_part, (row_start, key_column)
        )
        old_value = lax.dynamic_slice(buffer_now, (row_start, value_column), (block_rows, head_dim))
        buffer_now = lax.dynamic_update_slice(
            buffer_now, old_value + value_part, (row_start, value_column)
        )
        return (query_sum, buffer_now)

    start_query = jnp.zeros((rows, group_size, head_dim), jnp.float32)
    query_sum, backward_buffer = lax.fori_loop(0, needed, back_step, (start_query, backward_buffer))
    query_grads = [query_sum.astype(jnp.bfloat16)]
    grad_query_part = jnp.stack(query_grads, axis=1).reshape(
        rows, local_groups * group_size * head_dim
    )
    key_sums = lax.psum_scatter(
        backward_buffer.astype(jnp.bfloat16), "ctx", scatter_dimension=0, tiled=True
    ).astype(jnp.float32)
    grad_key = key_sums[:, : local_groups * head_dim].astype(jnp.bfloat16)
    grad_value = key_sums[:, local_groups * head_dim :].astype(jnp.bfloat16)
    squares_query = gram_pair_squares(hidden_gram, grad_query_part, head_dim)
    normal_size = D * head_dim * tok_dev
    fisher_q = jnp.log(squares_query / normal_size + EPSILON).reshape(1, -1)
    fisher_o = jnp.log(squares_out / normal_size + EPSILON).reshape(1, -1)
    return (grad_query_part, grad_key, grad_value, fisher_q, fisher_o)


def solution(mesh):
    return jax.shard_map(
        body,
        mesh=mesh,
        in_specs=(
            P("ctx", "head"),
            P("ctx", "head"),
            P("ctx", "head"),
            P("ctx", "head"),
            P("head", None),
            P("ctx", "head"),
            P("ctx"),
        ),
        out_specs=(
            P("ctx", "head"),
            P("ctx", "head"),
            P("ctx", "head"),
            P("ctx", "head"),
            P("ctx", "head"),
        ),
        check_vma=False,
    )
```

profile of v0, /device:TPU:0, one launch (start us, length us, event | category | flops | bytes accessed | tf_op | source)
XLA Modules:
  0.0 287.8 jit_solution(4906694200121494240)
XLA Ops:
  7.2 0.0 copy-start
  7.2 0.0 all-gather.3.cloned.1.call-start
  7.2 1.6 pad_maximum_fusion
  8.8 0.0 all-gather.3.cloned.1.call-update
  8.8 0.0 all-gather.5.cloned.1.call-start
  8.9 0.7 convert_add_fusion
  9.6 2.0 multiply_convert_fusion
  11.6 0.0 all-gather.5.cloned.1.call-update
  11.6 0.0 all-reduce.2.cloned.1.call-start
  11.6 0.0 copy-done
  11.6 1.0 fusion.64
  12.7 0.0 all-reduce.2.cloned.1.call-update
  12.7 0.0 reduce-scatter.2.cloned.1.call-start
  12.8 1.2 copy.18
  14.0 0.3 copy.22
  14.3 1.1 copy.21
  15.4 31.1 %all-gather.3.cloned.1.call-done = bf16[4096,256]{1,0:T(8,128)(2,1)} async-done(((bf16[256,256]{1,0:T(8,128)(2,1)}), bf16[4096,256]{1,0:T(8,128)(2,1)}) %all-gather.3.cloned.1.call-update) | async-done | bytes 2097168 | tf_op jit(solution)/shard_map/all_gather | solution.py:65
  46.4 2.7 fusion.62
  49.2 1.9 while.37
  49.2 0.1 broadcast_compare_fusion.6
  49.3 0.8 fusion.100
  50.1 0.9 exponential_reduce_fusion.2
  51.1 0.1 broadcast.137.clone
  51.1 3.0 %while.38 = (s32[]{:T(128)}, f32[256,8,128]{2,0,1:T(8,128)S(1)}, s32[]{:T(128)}, bf16[4096,128]{1,0:T(8,128)(2,1)S(1)}, bf16[256,8,128]{2,1,0:T(8,128)(2,1)}, /*...) while((s32[]{:T(128)}, f32[256,8,128]{2,0,1:T(8,128)S(1)}, ...), condition=%wide.region_5.6_spmd.clone, body=%wide.region_4.5_spmd.clone.sunk | while | flops 541459200 | bytes 3161259 | solution.py:112
  51.2 0.1 broadcast_compare_fusion.7
  51.3 2.8 fusion.104
  54.1 0.0 copy-start.1
  54.1 65.9 %all-gather.5.cloned.1.call-done = bf16[256,8192]{1,0:T(8,128)(2,1)} async-done(((bf16[256,1024]{1,0:T(8,128)(2,1)}), bf16[256,8192]{1,0:T(8,128)(2,1)}) %all-gather.5.cloned.1.call-update) | async-done | bytes 4194320 | tf_op jit(solution)/shard_map/all_gather | solution.py:121
  120.1 12.4 %fusion.59 = bf16[32,8,8,128]{3,2,1,0:T(8,128)(2,1)} fusion(bf16[256,8192]{1,0:T(8,128)(2,1)} %all-gather.5.cloned.1.call-done, bf16[1024,8192]{1,0:T(8,128)(2,1)} %param.17), kind=kOutput, calls=%fused_computation.65 | convolution fusion | flops 4295229440 | bytes 21495808 | tf_op jit(solution)/shard_map/dot_general | solution.py:122
  132.4 1.9 copy.36
  134.4 0.0 copy-done.1
  134.4 1.4 multiply_reduce_fusion.2
  135.8 0.1 broadcast.137
  135.8 2.2 broadcast_in_dim.50
  138.1 9.5 %while.39 = (s32[]{:T(128)}, f32[256,8,128]{2,0,1:T(8,128)S(1)}, f32[4096,256]{1,0:T(8,128)}, s32[]{:T(128)}, bf16[4096,128]{1,0:T(8,128)(2,1)S(1)}, /*index=5*/...) while((s32[]{:T(128)}, f32[256,8,128]{2,0,1:T(8,128)S(1)}, ...), condition=%wide.region_8.9_spmd.clone, body=%wide.region_7.8_spmd.clone.sunk | while | flops 1354236672 | bytes 27031796 | solution.py:178
  138.1 0.0 copy-start.3
  138.1 0.1 broadcast_compare_fusion.8
  138.2 0.7 fusion.115
  139.0 0.2 copy-done.3
  139.1 2.4 fusion.116
  141.5 0.9 convolution_add_fusion.2
  142.5 2.4 fusion.117
  144.9 2.7 fusion.118
  147.6 3.8 %convert_element_type.47 = bf16[4096,256]{1,0:T(8,128)(2,1)} convert(f32[4096,256]{1,0:T(8,128)} %get-tuple-element.150) | non-fusion elementwise | flops 1048576 | bytes 6291456 | tf_op jit(solution)/shard_map/convert_element_type | solution.py:184
  151.4 0.0 reduce-scatter.2.cloned.1.call-update
  151.4 0.0 copy-start.2
  151.4 4.8 %fusion.65 = f32[256,256]{1,0:T(8,128)S(1)} fusion(bf16[256,8192]{1,0:T(8,128)(2,1)} %all-gather.5.cloned.1.call-done), kind=kOutput, calls=%fused_computation.81 | convolution fusion | flops 1073741824 | bytes 4456448 | tf_op jit(solution)/shard_map/dot_general | solution.py:43
  156.2 0.0 copy-done.2
  156.3 0.5 multiply_reduce_fusion
  156.8 47.9 %all-reduce.2.cloned.1.call-done = f32[256,256]{1,0:T(8,128)} async-done(((f32[256,256]{1,0:T(8,128)}), f32[256,256]{1,0:T(8,128)}) %all-reduce.2.cloned.1.call-update) | async-done | bytes 262160 | tf_op jit(solution)/shard_map/psum | solution.py:59
  204.7 1.5 multiply_reduce_fusion.1
  206.2 0.5 log_bitcast_fusion
  206.7 0.5 log_bitcast_fusion.1
  207.2 0.9 copy_bitcast_fusion
  208.1 71.6 %reduce-scatter.2.cloned.1.call-done = bf16[256,256]{1,0:T(8,128)(2,1)} async-done(((bf16[4096,256]{1,0:T(8,128)(2,1)}), bf16[256,256]{1,0:T(8,128)(2,1)}) %reduce-scatter.2.cloned.1.call-update) | async-done | bytes 131088 | tf_op jit(solution)/shard_map/reduce_scatter | solution.py:183
  279.7 1.5 fusion.63
  (12 shorter events, 0.0 us)
Async XLA Ops:
  7.2 4.5 %copy-start = (bf16[256,1024]{1,0:T(8,128)(2,1)S(1)}, bf16[256,1024]{1,0:T(8,128)(2,1)}, u32[]{:S(2)}) copy-start(bf16[256,1024]{1,0:T(8,128)(2,1)} %param.13) | copy-start | bytes 1572868
  7.2 39.3 %all-gather.3.cloned.1.call-start = ((), (), s32[]{:S(2)}) async-start(), calls=%async_computation.1 | async-start | bytes 2228224 | tf_op jit(solution)/shard_map/all_gather | solution.py:65
  8.8 111.3 %all-gather.5.cloned.1.call-start = ((), (), s32[]{:S(2)}) async-start(), calls=%async_computation.2 | async-start | bytes 4718592 | tf_op jit(solution)/shard_map/all_gather | solution.py:121
  11.6 193.1 %all-reduce.2.cloned.1.call-start = ((), (), s32[]{:S(2)}) async-start(), calls=%async_computation.4 | async-start | bytes 524288 | tf_op jit(solution)/shard_map/psum | solution.py:59
  12.7 267.0 %reduce-scatter.2.cloned.1.call-start = ((), (), s32[]{:S(2)}) async-start(), calls=%async_computation.3 | async-start | bytes 2228224 | tf_op jit(solution)/shard_map/reduce_scatter | solution.py:183
  54.1 80.2 %copy-start.1 = (f32[256,8,128]{2,0,1:T(8,128)}, f32[256,8,128]{2,0,1:T(8,128)S(1)}, u32[]{:S(2)}) copy-start(f32[256,8,128]{2,0,1:T(8,128)S(1)} %get-tuple-element.148) | copy-start | bytes 3145732
  138.1 1.0 copy-start.3
  151.4 4.8 %copy-start.2 = (f32[256,8,128]{2,0,1:T(8,128)S(1)}, f32[256,8,128]{2,0,1:T(8,128)}, u32[]{:S(2)}) copy-start(f32[256,8,128]{2,0,1:T(8,128)} %copy-done.1) | copy-start | bytes 3145732
Sparse Core Ops, SparseCore 0:
  9.7 36.6 all-gather.2
  48.8 71.2 all-gather.4
  122.6 82.0 all-reduce.1
  207.1 72.5 reduce-scatter.1
where the time goes:
time: 289 us; the launch traced here: 288 us
  waiting for transfers between devices  217 us (75%)
  matrix products  33 us (11%)
  between operations  13.9 us (5%)
  other arithmetic  12.7 us (4%)
  local copies, waits for them, and re-layouts  11.4 us (4%)
    reduce_scatter x1, waiting for transfers between devices, body(): lax.psum_scatter(backward_buffer.astype(jnp.bfloat16), 'ctx', scatter_dim...  71.6 us
    all_gather x1, waiting for transfers between devices, body(): piece_part = lax.all_gather(weighted, 'head', axis=1, tiled=True)  65.9 us
    psum x1, waiting for transfers between devices, body(): lax.psum(lax.dot_general(hidden_in, hidden_in, (((1,), (1,)), ((), ())),...  47.9 us
    all_gather x1, waiting for transfers between devices, body(): lax.all_gather(jnp.concatenate([key_rows, value_rows], axis=1), 'ctx', ax...  31.1 us
    dot_general x1, matrix products, body(): lax.dot_general(piece_part, out_weight, (((1,), (1,)), ((), ())), preferr...  12.4 us
  transfers between devices with their start and end apart: 4, of which 4 were waited for; matrix products, arithmetic and copies ran while one was open for 19% of the time, Pallas kernels for 0%

commit v1 on v0

--- a/solution.py
+++ b/solution.py
@@ -62,9 +62,9 @@
         ),
         "head",
     )
-    pair_all = lax.all_gather(
-        jnp.concatenate([key_rows, value_rows], axis=1), "ctx", axis=0, tiled=True
-    )
+    x = jnp.concatenate([key_rows, value_rows], axis=1)
+    outgoing = jnp.stack([x] * lax.axis_size("ctx"))
+    pair_all = jnp.concatenate(lax.all_to_all(outgoing, "ctx", 0, 0), axis=0)
     kv_width = key_rows.shape[1]
     keys_all, values_all = (pair_all[:, :kv_width], pair_all[:, kv_width:])
     tokens = keys_all.shape[0]

time: 289 us -> 267 us (0.924)
  waiting for transfers between devices: 217 us -> 187 us
  starting transfers between devices: 0.16 us -> 6.68 us
    all_gather x1, waiting for transfers between devices: 65.9 us -> 29 us  [body(): piece_part = lax.all_gather(weighted, 'head', axis=1, tiled=True)]
    all_gather x1 -> x0, waiting for transfers between devices: 31.1 us -> none  [body(): lax.all_gather(jnp.concatenate([key_rows, value_rows], axis=1), 'ctx', ax...]
    all_to_all x0 -> x1, waiting for transfers between devices: none -> 30.7 us  [body(): pair_all = jnp.concatenate(lax.all_to_all(outgoing, 'ctx', 0, 0), axis=0)]
    reduce_scatter x1, waiting for transfers between devices: 71.6 us -> 79.8 us  [body(): lax.psum_scatter(backward_buffer.astype(jnp.bfloat16), 'ctx', scatter_dim...]
    all_to_all x0 -> x1, starting transfers between devices: none -> 6.56 us  [body(): pair_all = jnp.concatenate(lax.all_to_all(outgoing, 'ctx', 0, 0), axis=0)]
  transfers between devices with their start and end apart: 4 -> 4, of which waited for: 4 -> 4; matrix products, arithmetic and copies ran while one was open for 19% -> 20% of each run, Pallas kernels for 0% -> 0%
where the time goes in v1:
time: 267 us; the launch traced here: 265 us
  waiting for transfers between devices  187 us (70%)
  matrix products  33 us (12%)
  between operations  13.9 us (5%)
  other arithmetic  12.1 us (5%)
  local copies, waits for them, and re-layouts  11.9 us (4%)
  starting transfers between devices  6.68 us (3%)
    reduce_scatter x1, waiting for transfers between devices, body(): lax.psum_scatter(backward_buffer.astype(jnp.bfloat16), 'ctx', scatter_dim...  79.8 us
    psum x1, waiting for transfers between devices, body(): lax.psum(lax.dot_general(hidden_in, hidden_in, (((1,), (1,)), ((), ())),...  47.9 us
    all_to_all x1, waiting for transfers between devices, body(): pair_all = jnp.concatenate(lax.all_to_all(outgoing, 'ctx', 0, 0), axis=0)  30.7 us
    all_gather x1, waiting for transfers between devices, body(): piece_part = lax.all_gather(weighted, 'head', axis=1, tiled=True)  29 us
    dot_general x1, matrix products, body(): lax.dot_general(piece_part, out_weight, (((1,), (1,)), ((), ())), preferr...  12.4 us
    all_to_all x1, starting transfers between devices, body(): pair_all = jnp.concatenate(lax.all_to_all(outgoing, 'ctx', 0, 0), axis=0)  6.56 us
  transfers between devices with their start and end apart: 4, of which 4 were waited for; matrix products, arithmetic and copies ran while one was open for 20% of the time, Pallas kernels for 0%

profile of v1, /device:TPU:0, one launch (start us, length us, event | category | flops | bytes accessed | tf_op | source)
XLA Modules:
  0.0 265.1 jit_solution(16065485428916227721)
XLA Ops:
  7.2 0.0 copy-start
  7.2 0.0 all-gather.2.cloned.1.call-start
  7.2 0.7 convert_add_fusion
  8.0 2.0 multiply_convert_fusion
  9.9 0.0 all-gather.2.cloned.1.call-update
  10.0 0.0 copy-start.3
  10.0 0.9 pad_maximum_fusion
  10.9 1.5 stack.2
  12.5 6.6 %all-to-all-start = ((bf16[16,256,256]{2,1,0:T(8,128)(2,1)}), bf16[16,256,256]{2,1,0:T(8,128)(2,1)}, u32[]{:S(2)}, u32[]{:S(2)}) async-start(bf16[16,256,256]{2,1,0:T(8,128)(2,1)} %stack.2), calls=%async_computation | async-start | bytes 4194304 | tf_op jit(solution)/shard_map/all_to_all | solution.py:67
  19.0 0.0 all-reduce.2.cloned.1.call-start
  19.1 0.0 copy-done
  19.1 1.0 fusion.64
  20.1 0.0 all-reduce.2.cloned.1.call-update
  20.2 0.0 reduce-scatter.2.cloned.1.call-start
  20.2 0.0 copy-done.3
  20.2 0.2 copy.18
  20.4 0.3 copy.22
  20.7 1.1 copy.21
  21.8 30.7 %all-to-all-done = bf16[16,256,256]{2,1,0:T(8,128)(2,1)} async-done(((bf16[16,256,256]{2,1,0:T(8,128)(2,1)}), bf16[16,256,256]{2,1,0:T(8,128)(2,1)}, u32[]{:S(2)}, u32[]{:S(2)}) %all-to-all-start) | async-done | bytes 2097184 | tf_op jit(solution)/shard_map/all_to_all | solution.py:67
  52.5 2.8 %fusion.62 = (bf16[4096,128]{1,0:T(8,128)(2,1)}, bf16[4096,128]{1,0:T(8,128)(2,1)S(1)}) fusion(bf16[4096,256]{1,0:T(8,128)(2,1)} %bitcast), kind=kLoop, calls=%fused_computation.78 | loop fusion | bytes 4194304 | tf_op jit(solution)/shard_map/slice | solution.py:69
  55.3 1.9 while.37
  55.3 0.1 broadcast_compare_fusion.6
  55.5 0.8 fusion.100
  56.3 0.9 exponential_reduce_fusion.2
  57.2 0.1 broadcast.139.clone
  57.3 3.0 %while.38 = (s32[]{:T(128)}, f32[256,8,128]{2,0,1:T(8,128)S(1)}, s32[]{:T(128)}, bf16[4096,128]{1,0:T(8,128)(2,1)S(1)}, bf16[256,8,128]{2,1,0:T(8,128)(2,1)}, /*...) while((s32[]{:T(128)}, f32[256,8,128]{2,0,1:T(8,128)S(1)}, ...), condition=%wide.region_5.6_spmd.clone, body=%wide.region_4.5_spmd.clone.sunk | while | flops 541459200 | bytes 3161259 | solution.py:112
  57.3 0.1 broadcast_compare_fusion.7
  57.5 2.8 %fusion.104 = f32[256,8,128]{2,0,1:T(8,128)S(1)} fusion(f32[256,8,128]{2,0,1:T(8,128)S(1)} %get-tuple-element.530, f32[256,8]{0,1:T(8,128)S(1)} %get-tuple-element.546, pred[256,512]{1,0:T(8,128)(4,1)S(1)} %broadcast_compare_fusion.7, bf16[256,8,128]{2,1,0:T(8,128)(2,1)} %get-tuple-element.545, bf16[4096,128]{1,0:T(8,128)(2,1)} %get-tuple-element.547, ...), kind=kOutput, calls=%fused_computation.19.clone.1 | convolution fusion | flops 541327360 | bytes 3023872 | tf_op jit(solution)/shard_map/while/body/tgk,kd->tgd/dot_general | solution.py:108
  60.3 0.0 copy-start.1
  60.3 29.0 %all-gather.2.cloned.1.call-done = bf16[256,8192]{1,0:T(8,128)(2,1)} async-done(((bf16[256,1024]{1,0:T(8,128)(2,1)}), bf16[256,8192]{1,0:T(8,128)(2,1)}) %all-gather.2.cloned.1.call-update) | async-done | bytes 4194320 | tf_op jit(solution)/shard_map/all_gather | solution.py:121
  89.2 12.4 %fusion.59 = bf16[32,8,8,128]{3,2,1,0:T(8,128)(2,1)} fusion(bf16[256,8192]{1,0:T(8,128)(2,1)} %all-gather.2.cloned.1.call-done, bf16[1024,8192]{1,0:T(8,128)(2,1)} %param.17), kind=kOutput, calls=%fused_computation.65 | convolution fusion | flops 4295229440 | bytes 21495808 | tf_op jit(solution)/shard_map/dot_general | solution.py:122
  101.6 1.9 copy.36
  103.5 0.0 copy-done.1
  103.5 1.4 multiply_reduce_fusion.2
  104.9 0.1 broadcast.139
  105.0 2.2 broadcast_in_dim.50
  107.2 9.5 %while.39 = (s32[]{:T(128)}, f32[256,8,128]{2,0,1:T(8,128)S(1)}, f32[4096,256]{1,0:T(8,128)}, s32[]{:T(128)}, bf16[4096,128]{1,0:T(8,128)(2,1)S(1)}, /*index=5*/...) while((s32[]{:T(128)}, f32[256,8,128]{2,0,1:T(8,128)S(1)}, ...), condition=%wide.region_8.9_spmd.clone, body=%wide.region_7.8_spmd.clone.sunk | while | flops 1354236672 | bytes 27031796 | solution.py:178
  107.2 0.0 copy-start.4
  107.2 0.1 broadcast_compare_fusion.8
  107.4 0.7 fusion.115
  108.1 0.2 copy-done.4
  108.3 2.4 fusion.116
  110.7 0.9 convolution_add_fusion.2
  111.6 2.4 fusion.117
  114.0 2.7 %fusion.118 = f32[4096,256]{1,0:T(8,128)} fusion(f32[4096,256]{1,0:T(8,128)} %fusion.117, s32[]{:T(128)S(6)} %select_n.85, bf16[256,8,128]{2,0,1:T(8,128)(2,1)S(1)} %copy-done.4, f32[512,256,8]{1,0,2:T(8,128)S(1)} %fusion.115, f32[256,8]{0,1:T(8,128)S(1)} %get-tuple-element.589, pred[256,512]{0,1:T(8,128)(4,1)S(1)} %broadcast_compare_fusion.8), kind=kOutput, calls=%fused_computation.44.clone.1 | convolution fusion | flops 272695296 | bytes 5382148 | tf_op jit(solution)/shard_map/while/body/tgk,tgd->kd/dot_general | solution.py:163
  116.8 3.8 %convert_element_type.47 = bf16[4096,256]{1,0:T(8,128)(2,1)} convert(f32[4096,256]{1,0:T(8,128)} %get-tuple-element.150) | non-fusion elementwise | flops 1048576 | bytes 6291456 | tf_op jit(solution)/shard_map/convert_element_type | solution.py:184
  120.5 0.0 reduce-scatter.2.cloned.1.call-update
  120.6 0.0 copy-start.2
  120.6 4.8 %fusion.65 = f32[256,256]{1,0:T(8,128)S(1)} fusion(bf16[256,8192]{1,0:T(8,128)(2,1)} %all-gather.2.cloned.1.call-done), kind=kOutput, calls=%fused_computation.81 | convolution fusion | flops 1073741824 | bytes 4456448 | tf_op jit(solution)/shard_map/dot_general | solution.py:43
  125.4 0.0 copy-done.2
  125.4 0.5 multiply_reduce_fusion
  126.0 47.9 %all-reduce.2.cloned.1.call-done = f32[256,256]{1,0:T(8,128)} async-done(((f32[256,256]{1,0:T(8,128)}), f32[256,256]{1,0:T(8,128)}) %all-reduce.2.cloned.1.call-update) | async-done | bytes 262160 | tf_op jit(solution)/shard_map/psum | solution.py:59
  173.8 1.5 multiply_reduce_fusion.1
  175.3 0.5 log_bitcast_fusion
  175.8 0.5 log_bitcast_fusion.1
  176.4 0.9 copy_bitcast_fusion
  177.2 79.8 %reduce-scatter.2.cloned.1.call-done = bf16[256,256]{1,0:T(8,128)(2,1)} async-done(((bf16[4096,256]{1,0:T(8,128)(2,1)}), bf16[256,256]{1,0:T(8,128)(2,1)}) %reduce-scatter.2.cloned.1.call-update) | async-done | bytes 131088 | tf_op jit(solution)/shard_map/reduce_scatter | solution.py:183
  257.0 1.5 fusion.63
  (12 shorter events, 0.0 us)
Async XLA Ops:
  7.2 11.9 %copy-start = (bf16[256,1024]{1,0:T(8,128)(2,1)S(1)}, bf16[256,1024]{1,0:T(8,128)(2,1)}, u32[]{:S(2)}) copy-start(bf16[256,1024]{1,0:T(8,128)(2,1)} %param.13) | copy-start | bytes 1572868
  7.2 82.0 %all-gather.2.cloned.1.call-start = ((), (), s32[]{:S(2)}) async-start(), calls=%async_computation.2 | async-start | bytes 4718592 | tf_op jit(solution)/shard_map/all_gather | solution.py:121
  10.0 10.2 %copy-start.3 = (bf16[256,1024]{1,0:T(8,128)(2,1)S(1)}, bf16[256,1024]{1,0:T(8,128)(2,1)}, u32[]{:S(2)}) copy-start(bf16[256,1024]{1,0:T(8,128)(2,1)} %param.14) | copy-start | bytes 1572868
  12.5 40.0 %all-to-all-start = ((bf16[16,256,256]{2,1,0:T(8,128)(2,1)}), bf16[16,256,256]{2,1,0:T(8,128)(2,1)}, u32[]{:S(2)}, u32[]{:S(2)}) async-start(bf16[16,256,256]{2,1,0:T(8,128)(2,1)} %stack.2), calls=%async_computation | async-start | bytes 4194304 | tf_op jit(solution)/shard_map/all_to_all | solution.py:67
  19.0 154.8 %all-reduce.2.cloned.1.call-start = ((), (), s32[]{:S(2)}) async-start(), calls=%async_computation.4 | async-start | bytes 524288 | tf_op jit(solution)/shard_map/psum | solution.py:59
  20.2 236.8 %reduce-scatter.2.cloned.1.call-start = ((), (), s32[]{:S(2)}) async-start(), calls=%async_computation.3 | async-start | bytes 2228224 | tf_op jit(solution)/shard_map/reduce_scatter | solution.py:183
  60.3 43.3 %copy-start.1 = (f32[256,8,128]{2,0,1:T(8,128)}, f32[256,8,128]{2,0,1:T(8,128)S(1)}, u32[]{:S(2)}) copy-start(f32[256,8,128]{2,0,1:T(8,128)S(1)} %get-tuple-element.148) | copy-start | bytes 3145732
  107.2 1.0 copy-start.4
  120.6 4.8 %copy-start.2 = (f32[256,8,128]{2,0,1:T(8,128)S(1)}, f32[256,8,128]{2,0,1:T(8,128)}, u32[]{:S(2)}) copy-start(f32[256,8,128]{2,0,1:T(8,128)} %copy-done.1) | copy-start | bytes 3145732
Sparse Core Ops, SparseCore 0:
  10.4 78.8 all-gather.1
  91.7 82.0 all-reduce.1
  176.3 80.6 reduce-scatter.1
